TPU v7x, 1024 devices: a whole 4x8x16 slice. The times are simulated.
1024 devices in a mesh: dp: 128 (over z, y_hi, core), fsdp: 8 (over y_lo, x).
Axes of the slice: x: 4, y: 8 (y_hi: 4, y_lo: 2; y = y_hi * 2 + y_lo), z: 16, core: 2. Of those that a mesh axis runs over, the one named last changes fastest.
Arguments:
- tokens: bfloat16 [16384, 3072], P('dp', 'fsdp'), may hold values from -6 to 6
- weight_blocks: bfloat16 [96, 3, 128, 128], P('fsdp'), may hold values from -0.3125 to 0.3125
- pattern: int32 [96, 3], P('fsdp'), may hold values from 0 to 23, as said below
- grad_out: bfloat16 [16384, 12288], P('dp', 'fsdp'), may hold values from -6 to 6
Outputs:
- projected: bfloat16 [16384, 12288], P('dp', 'fsdp')
- grad_tokens: bfloat16 [16384, 3072], P('dp', 'fsdp')
- grad_weight: float32 [96, 3, 16384], P('fsdp', None, 'dp')
Inputs may be any that keep to these rules, and one draw needn't show every extreme that they name: `pattern`: each block-column names 3 different block-rows; every block-row is named by exactly 12 block-columns.
All inputs are finite; a program needn't handle non-finite values.
Results may differ from a plain program's by a relative error of at most 0.001.
Values may be sent and summed in bfloat16 or wider, within the bound.
No kernel may reach another device: no remote copies, remote signals or barrier semaphores. Data moves between devices by JAX's collectives and lax.ppermute only.
A program may use at most 32 MiB of HBM per device.

v0:
```python
import jax
import jax.numpy as jnp
from jax import lax
from jax.sharding import PartitionSpec as P


def on_device(tokens, weight_blocks, pattern, grad_out):
    count_rows = tokens.shape[0]
    columns, slots, block_size = (
        weight_blocks.shape[0],
        weight_blocks.shape[1],
        weight_blocks.shape[3],
    )
    whole = lax.all_gather(tokens, "fsdp", axis=1, tiled=True)
    width = whole.shape[1]
    row_blocks = width // block_size
    whole_rows = whole.reshape(count_rows, row_blocks, block_size)
    grad_cols = grad_out.reshape(count_rows, columns, block_size)
    row_ids = jnp.arange(row_blocks, dtype=jnp.int32)
    projected_sum = jnp.zeros((count_rows, columns, block_size), jnp.float32)
    partial_grads = jnp.zeros((count_rows, row_blocks, block_size), jnp.float32)
    slot_terms = []
    for slot in range(slots):
        selector = row_ids[:, None] == pattern[:, slot][None, :]
        picked_slot = jnp.einsum(
            "trb,rc->tcb",
            whole_rows,
            selector.astype(jnp.bfloat16),
            preferred_element_type=jnp.float32,
        ).astype(jnp.bfloat16)
        weight_slot = weight_blocks[:, slot]
        projected_sum = projected_sum + jnp.einsum(
            "tcb,cbo->tco", picked_slot, weight_slot, preferred_element_type=jnp.float32
        )
        backward_slot = jnp.einsum(
            "tco,cbo->tcb", grad_cols, weight_slot, preferred_element_type=jnp.float32
        )
        partial_grads = partial_grads + jnp.einsum(
            "tcb,rc->trb",
            backward_slot,
            selector.astype(jnp.float32),
            precision=lax.Precision.HIGHEST,
        )
        slot_terms.append(
            jnp.einsum(
                "tcb,tco->cbo", picked_slot, grad_cols, preferred_element_type=jnp.float32
            ).reshape(columns, block_size * block_size)
        )
    projected = projected_sum.astype(jnp.bfloat16).reshape(count_rows, columns * block_size)
    partial_grads = partial_grads.reshape(count_rows, width)
    grad_tokens = lax.psum_scatter(partial_grads, "fsdp", scatter_dimension=1, tiled=True).astype(
        jnp.bfloat16
    )
    scale_factor = 1.0 / jnp.sqrt(jnp.float32(count_rows * lax.axis_size("dp")))
    weight_terms = jnp.stack(slot_terms, axis=1)
    grad_weight = (
        lax.psum_scatter(weight_terms, "dp", scatter_dimension=2, tiled=True) * scale_factor
    )
    return (projected, grad_tokens, grad_weight)


def solution(mesh):
    placed = (P("dp", "fsdp"), P("fsdp", None, None, None), P("fsdp", None), P("dp", "fsdp"))
    return jax.shard_map(
        on_device,
        mesh=mesh,
        in_specs=placed,
        out_specs=(P("dp", "fsdp"), P("dp", "fsdp"), P("fsdp", None, "dp")),
        check_vma=False,
    )
```

profile of v0, /device:TPU:6, one launch (start us, length us, event | category | flops | bytes accessed | tf_op | source)
XLA Modules:
  0.0 357.4 jit_solution(17913662587662626728)
XLA Ops:
  7.2 1.3 copy.29
  8.5 1.3 fusion.9
  9.8 1.2 fusion.12
  11.3 1.4 copy.40
  12.7 1.6 copy.39
  14.3 1.4 copy.38
  15.7 0.9 fusion.5
  16.9 0.9 fusion.7
  17.9 1.0 add_add_fusion
  19.0 1.4 copy.50
  20.5 0.8 copy-done.10
  21.3 37.0 %all_gather.3 = bf16[128,3072]{1,0:T(8,128)(2,1)S(1)} all-gather(bf16[128,384]{1,0:T(8,128)(2,1)S(1)} %copy-done.10), channel_id=1, replica_groups=mesh['dp'=128,'fsdp'=8] {'fsdp'}, dimensions={1}, use_global_device_ids=true | all-gather | bytes 884736 | tf_op jit(solution)/shard_map/all_gather | solution.py:14
  58.5 0.4 fusion.3
  58.9 1.1 copy.34
  60.0 0.3 fusion.1
  60.3 1.1 copy.30
  61.8 0.4 copy.32
  62.2 1.3 fusion.41
  63.5 1.3 stack_reshape.10
  64.8 1.3 fusion.40
  66.1 2.3 stack_reshape.9
  68.4 1.3 fusion.42
  69.8 2.4 stack_reshape.11
  72.1 3.1 pad_maximum_fusion
  75.2 1.0 copy-done.7
  76.5 0.7 copy-done.5
  77.5 0.7 copy-done.9
  78.5 0.9 copy.36
  79.5 1.6 convert_element_type.41
  81.1 268.2 %reduce-scatter.5.cloned.1.call-done = f32[12,3,128]{2,0,1:T(8,128)} async-done(((f32[12,3,16384]{2,0,1:T(8,128)}), f32[12,3,128]{2,0,1:T(8,128)}) %reduce-scatter.5.cloned.1.call-update) | async-done | bytes 18448 | tf_op jit(solution)/shard_map/reduce_scatter | solution.py:57
  349.2 0.7 broadcast_multiply_fusion
  349.9 0.6 copy.37
  (32 shorter events, 2.2 us)
Async XLA Ops:
  7.2 2.6 copy-start
  7.2 72.3 %reduce-scatter.3.cloned.1.call-start = ((), (), s32[]{:S(2)}) async-start(), calls=%async_computation.2 | async-start | bytes 1769472 | tf_op jit(solution)/shard_map/reduce_scatter | solution.py:51
  9.8 1.5 copy-start.11
  15.7 1.2 copy-start.1
  16.6 1.3 copy-start.2
  20.4 0.9 copy-start.10
  20.4 328.8 %reduce-scatter.5.cloned.1.call-start = ((), (), s32[]{:S(2)}) async-start(), calls=%async_computation.3 | async-start | bytes 3170304 | tf_op jit(solution)/shard_map/reduce_scatter | solution.py:57
  62.2 2.6 copy-start.4
  62.2 2.6 copy-start.6
  66.1 2.3 copy-start.8
  69.8 2.4 copy-start.3
  75.2 1.0 copy-start.7
  76.2 1.0 copy-start.5
  77.2 1.0 copy-start.9
Sparse Core Ops, SparseCore 0:
  20.5 57.7 reduce-scatter.2
  84.2 264.9 reduce-scatter.4
where the time goes:
time: 358 us; the launch traced here: 357 us
  waiting for transfers between devices  268 us (75%)
  blocking collectives  37 us (10%)
  local copies, waits for them, and re-layouts  21 us (6%)
  between operations  14.2 us (4%)
  matrix products  11.5 us (3%)
  other arithmetic  5.4 us (2%)
    reduce_scatter x1, waiting for transfers between devices, on_device(): lax.psum_scatter(weight_terms, 'dp', scatter_dimension=2, tiled=True)  268 us
    all_gather x1, blocking collectives, on_device(): whole = lax.all_gather(tokens, 'fsdp', axis=1, tiled=True)  37 us
    unnamed x29, local copies, waits for them, and re-layouts  8 us
  transfers between devices with their start and end apart: 2, of which 1 were waited for; matrix products, arithmetic and copies ran while one was open for 6% of the time, Pallas kernels for 0%

commit v1 on v0

--- a/solution.py
+++ b/solution.py
@@ -1,7 +1,25 @@
 import jax
 import jax.numpy as jnp
 from jax import lax
+from jax.sharding import Mesh
 from jax.sharding import PartitionSpec as P
+
+DP_SPLIT = (("z", 16), ("yh", 4), ("c", 2))
+DP = tuple(name for name, _ in DP_SPLIT)
+
+
+def reduce_over_dp(terms):
+    rows, width = terms.shape
+    pairs = terms.reshape(rows // 2, 2, width)
+    mine = lax.axis_index("c")
+    keep = lax.dynamic_index_in_dim(pairs, mine, axis=1, keepdims=False)
+    send = lax.dynamic_index_in_dim(pairs, 1 - mine, axis=1, keepdims=False)
+    halved = keep + lax.ppermute(send, "c", [(0, 1), (1, 0)])
+    planes, lanes = DP_SPLIT[0][1], DP_SPLIT[1][1]
+    across = halved.reshape(planes, lanes, width).transpose(1, 0, 2).reshape(lanes, planes * width)
+    across = jnp.sum(lax.all_to_all(across, "yh", 0, 0, tiled=True), axis=0)
+    along = lax.all_to_all(across.reshape(planes, width), "z", 0, 0, tiled=True)
+    return jnp.sum(along, axis=0)
 
 
 def on_device(tokens, weight_blocks, pattern, grad_out):
@@ -42,29 +60,29 @@
             precision=lax.Precision.HIGHEST,
         )
         slot_terms.append(
-            jnp.einsum(
-                "tcb,tco->cbo", picked_slot, grad_cols, preferred_element_type=jnp.float32
-            ).reshape(columns, block_size * block_size)
+            jnp.einsum("tcb,tco->bco", picked_slot, grad_cols, preferred_element_type=jnp.float32)
         )
     projected = projected_sum.astype(jnp.bfloat16).reshape(count_rows, columns * block_size)
     partial_grads = partial_grads.reshape(count_rows, width)
     grad_tokens = lax.psum_scatter(partial_grads, "fsdp", scatter_dimension=1, tiled=True).astype(
         jnp.bfloat16
     )
-    scale_factor = 1.0 / jnp.sqrt(jnp.float32(count_rows * lax.axis_size("dp")))
-    weight_terms = jnp.stack(slot_terms, axis=1)
-    grad_weight = (
-        lax.psum_scatter(weight_terms, "dp", scatter_dimension=2, tiled=True) * scale_factor
-    )
+    scale_factor = 1.0 / jnp.sqrt(jnp.float32(count_rows * lax.axis_size(DP)))
+    weight_terms = jnp.stack(slot_terms, axis=2).reshape(block_size, columns * slots * block_size)
+    grad_weight = reduce_over_dp(weight_terms).reshape(columns, slots, block_size) * scale_factor
     return (projected, grad_tokens, grad_weight)
 
 
 def solution(mesh):
-    placed = (P("dp", "fsdp"), P("fsdp", None, None, None), P("fsdp", None), P("dp", "fsdp"))
+    split = Mesh(
+        mesh.devices.reshape(tuple(size for _, size in DP_SPLIT) + (mesh.shape["fsdp"],)),
+        DP + ("fsdp",),
+    )
+    placed = (P(DP, "fsdp"), P("fsdp", None, None, None), P("fsdp", None), P(DP, "fsdp"))
     return jax.shard_map(
         on_device,
-        mesh=mesh,
+        mesh=split,
         in_specs=placed,
-        out_specs=(P("dp", "fsdp"), P("dp", "fsdp"), P("fsdp", None, "dp")),
+        out_specs=(P(DP, "fsdp"), P(DP, "fsdp"), P("fsdp", None, DP)),
         check_vma=False,
     )

time: 358 us -> 166 us (0.46)
  waiting for transfers between devices: 268 us -> 13.4 us
  blocking collectives: 37 us -> 75 us
  starting transfers between devices: 0.08 us -> 23.4 us
  local copies, waits for them, and re-layouts: 21 us -> 25.3 us
  matrix products: 11.5 us -> 7.65 us
    reduce_scatter x1 -> x0, waiting for transfers between devices: 268 us -> none  [on_device(): lax.psum_scatter(weight_terms, 'dp', scatter_dimension=2, tiled=True)]
    all_to_all x0 -> x1, blocking collectives: none -> 38.3 us  [reduce_over_dp(): across = jnp.sum(lax.all_to_all(across, 'yh', 0, 0, tiled=True), axis=0)]
    all_to_all x0 -> x1, starting transfers between devices: none -> 21.3 us  [reduce_over_dp(): along = lax.all_to_all(across.reshape(planes, width), 'z', 0, 0, tiled=True)]
    all_to_all x0 -> x1, waiting for transfers between devices: none -> 13.4 us  [reduce_over_dp(): along = lax.all_to_all(across.reshape(planes, width), 'z', 0, 0, tiled=True)]
    transpose x0 -> x3, local copies, waits for them, and re-layouts: none -> 5.28 us  [on_device(): jnp.einsum('tco,cbo->tcb', grad_cols, weight_slot, preferred_element_type...]
    dynamic_slice x0 -> x1, local copies, waits for them, and re-layouts: none -> 4.8 us  [reduce_over_dp(): keep = lax.dynamic_index_in_dim(pairs, mine, axis=1, keepdims=False)]
    dot_general x3 -> x0, local copies, waits for them, and re-layouts: 4.4 us -> none  [on_device(): jnp.einsum('tco,cbo->tcb', grad_cols, weight_slot, preferred_element_type...]
    unnamed x29 -> x27, local copies, waits for them, and re-layouts: 8 us -> 6.2 us
  transfers between devices with their start and end apart: 2 -> 3, of which waited for: 1 -> 1; matrix products, arithmetic and copies ran while one was open for 6% -> 12% of each run, Pallas kernels for 0% -> 0%
where the time goes in v1:
time: 166 us; the launch traced here: 165 us
  blocking collectives  75 us (45%)
  local copies, waits for them, and re-layouts  25.3 us (15%)
  starting transfers between devices  23.4 us (14%)
  between operations  14.3 us (9%)
  waiting for transfers between devices  13.4 us (8%)
  matrix products  7.65 us (5%)
  other arithmetic  5.54 us (3%)
    all_to_all x1, blocking collectives, reduce_over_dp(): across = jnp.sum(lax.all_to_all(across, 'yh', 0, 0, tiled=True), axis=0)  38.3 us
    all_gather x1, blocking collectives, on_device(): whole = lax.all_gather(tokens, 'fsdp', axis=1, tiled=True)  36.7 us
    all_to_all x1, starting transfers between devices, reduce_over_dp(): along = lax.all_to_all(across.reshape(planes, width), 'z', 0, 0, tiled=True)  21.3 us
    all_to_all x1, waiting for transfers between devices, reduce_over_dp(): along = lax.all_to_all(across.reshape(planes, width), 'z', 0, 0, tiled=True)  13.4 us
    unnamed x27, local copies, waits for them, and re-layouts  6.2 us
    transpose x3, local copies, waits for them, and re-layouts, on_device(): jnp.einsum('tco,cbo->tcb', grad_cols, weight_slot, preferred_element_type...  5.28 us
    dynamic_slice x1, local copies, waits for them, and re-layouts, reduce_over_dp(): keep = lax.dynamic_index_in_dim(pairs, mine, axis=1, keepdims=False)  4.8 us
  transfers between devices with their start and end apart: 3, of which 1 were waited for; matrix products, arithmetic and copies ran while one was open for 12% of the time, Pallas kernels for 0%

profile of v1, /device:TPU:6, one launch (start us, length us, event | category | flops | bytes accessed | tf_op | source)
XLA Modules:
  0.0 164.6 jit_solution(9443312087086066331)
XLA Ops:
  7.2 0.8 slice_bitcast_fusion
  8.0 1.2 copy.115
  9.2 36.7 %all_gather.3 = bf16[128,3072]{1,0:T(8,128)(2,1)S(1)} all-gather(bf16[128,384]{1,0:T(8,128)(2,1)} %param.4), channel_id=1, replica_groups=mesh['z'=16,'yh'=4,'c'=2,'fsdp'=8] {'fsdp'}, dimensions={1}, use_global_device_ids=true | all-gather | bytes 884736 | tf_op jit(solution)/shard_map/all_gather | solution.py:32
  46.4 0.4 copy.129
  47.5 0.4 copy.125
  47.9 0.4 copy.127
  48.3 0.4 convolution_bitcast_fusion.1
  48.7 0.4 convolution_bitcast_fusion
  49.1 0.4 convolution_bitcast_fusion.2
  49.8 1.6 copy.131
  51.4 3.3 %reshape_reshape.3 = f32[64,2,4608]{2,1,0:T(2,128)} reshape(f32[128,12,3,128]{3,2,1,0:T(4,128)S(1)} %copy.131) | data formatting | bytes 4718592 | tf_op jit(solution)/shard_map/reshape;reshape | solution.py:13
  54.7 4.8 %constant_dynamic-slice_fusion.1 = (f32[64,1,4608]{2,1,0:T(1,128)S(1)}, f32[64,1,4608]{2,1,0:T(1,128)S(1)}) fusion(f32[64,2,4608]{2,1,0:T(2,128)} %reshape_reshape.3, s32[]{:T(128)S(6)} %select_n.7, s32[]{:T(128)S(6)} %select_n.8), kind=kLoop, calls=%fused_computation.49 | loop fusion | bytes 4718600 | tf_op jit(solution)/shard_map/jit(dynamic_index_in_dim)/dynamic_slice | solution.py:15
  59.5 1.1 copy.156
  60.6 2.1 %collective-permute-start = (f32[64,4608]{1,0:T(8,128)}, f32[64,4608]{1,0:T(8,128)}, u32[]{:S(2)}, u32[]{:S(2)}) collective-permute-start(f32[64,4608]{1,0:T(8,128)} %bitcast.100), channel_id=1, source_target_pairs={{0,8},{8,0},{1,9},{9,1},{2,10},{10,2},{3,11},{11,3},{4,12},{12,4},... | collective-permute-start | bytes 3538952 | tf_op jit(solution)/shard_map/ppermute | solution.py:17
  62.7 1.1 convolution_bitcast_fusion.3
  64.1 2.5 %copy.124 = f32[128,12,128]{2,1,0:T(8,128)} copy(f32[128,12,128]{0,2,1:T(8,128)} %convolution_bitcast_fusion.3) | data formatting | bytes 1572864 | tf_op jit(solution)/shard_map/tco,cbo->tcb/transpose | solution.py:53
  66.6 1.4 copy.121
  68.3 1.4 copy.118
  69.7 0.9 fusion.22
  70.9 0.9 fusion.18
  72.1 1.0 add_add_fusion
  73.2 1.4 copy.155
  74.6 1.4 bitcast_add_fusion
  76.4 1.2 copy.132
  77.6 38.3 %all_to_all.18 = f32[4,1,73728]{2,1,0:T(1,128)S(1)} all-to-all(f32[4,1,73728]{2,1,0:T(1,128)S(1)} %copy.132), channel_id=1, replica_groups=mesh['z'=16,'yh'=4,'c'=2,'fsdp'=8] {'yh'}, dimensions={0} | all-to-all | bytes 2359296 | tf_op jit(solution)/shard_map/all_to_all | solution.py:20
  116.0 2.1 %reduce_sum.18 = f32[73728]{0:T(1024)} reduce(f32[4,1,73728]{2,1,0:T(1,128)S(1)} %all_to_all.18, f32[]{:T(128)} %constant.20.clone.1), dimensions={0,1}, to_apply=%region_1.2 | reduce | flops 221184 | bytes 1474564 | tf_op jit(solution)/shard_map/reduce_sum | solution.py:20
  118.1 21.3 %all-to-all-start.1 = ((f32[16,1,4608]{2,1,0:T(1,128)}), f32[16,1,4608]{2,1,0:T(1,128)S(1)}, u32[]{:S(2)}, u32[]{:S(2)}) async-start(f32[16,1,4608]{2,1,0:T(1,128)} %bitcast.27), calls=%async_computation.2 | async-start | bytes 589824 | tf_op jit(solution)/shard_map/all_to_all | solution.py:21
  140.1 0.7 copy-done.10
  141.1 0.9 copy.134
  142.0 1.6 convert_element_type.41
  143.6 13.4 %all-to-all-done.1 = f32[16,1,4608]{2,1,0:T(1,128)S(1)} async-done(((f32[16,1,4608]{2,1,0:T(1,128)}), f32[16,1,4608]{2,1,0:T(1,128)S(1)}, u32[]{:S(2)}, u32[]{:S(2)}) %all-to-all-start.1) | async-done | bytes 294944 | tf_op jit(solution)/shard_map/all_to_all | solution.py:21
  157.2 0.6 mul.11
  (38 shorter events, 4.2 us)
Async XLA Ops:
  7.2 134.8 %reduce-scatter.2.cloned.1.call-start = ((), (), s32[]{:S(2)}) async-start(), calls=%async_computation.3 | async-start | bytes 1769472 | tf_op jit(solution)/shard_map/reduce_scatter | solution.py:67
  46.8 1.9 %copy-start.9 = (bf16[128,12,128]{0,2,1:T(8,128)(2,1)}, bf16[128,12,128]{0,2,1:T(8,128)(2,1)S(1)}, u32[]{:S(2)}) copy-start(bf16[128,12,128]{0,2,1:T(8,128)(2,1)S(1)} %copy.129) | copy-start | bytes 1179652
  47.9 1.2 copy-start.7
  48.3 0.8 copy-start.5
  59.5 3.3 %copy-start = (bf16[12,3,128,128]{3,2,1,0:T(8,128)(2,1)S(1)}, bf16[12,3,128,128]{3,2,1,0:T(8,128)(2,1)}, u32[]{:S(2)}) copy-start(bf16[12,3,128,128]{3,2,1,0:T(8,128)(2,1)} %param.5) | copy-start | bytes 3538948
  60.6 14.0 %collective-permute-start = (f32[64,4608]{1,0:T(8,128)}, f32[64,4608]{1,0:T(8,128)}, u32[]{:S(2)}, u32[]{:S(2)}) collective-permute-start(f32[64,4608]{1,0:T(8,128)} %bitcast.100), channel_id=1, source_target_pairs={{0,8},{8,0},{1,9},{9,1},{2,10},{10,2},{3,11},{11,3},{4,12},{12,4},... | collective-permute-start | bytes 3538952 | tf_op jit(solution)/shard_map/ppermute | solution.py:17
  68.3 1.4 copy-start.2
  69.7 1.2 copy-start.3
  70.9 1.2 copy-start.4
  116.0 23.4 %copy-start.1 = (bf16[12,3,128,128]{3,2,1,0:T(8,128)(2,1)S(1)}, bf16[12,3,128,128]{3,2,1,0:T(8,128)(2,1)}, u32[]{:S(2)}) copy-start(bf16[12,3,128,128]{3,2,1,0:T(8,128)(2,1)} %param.5) | copy-start | bytes 3538948
  116.0 23.4 %copy-start.8 = (bf16[128,12,128]{0,2,1:T(8,128)(2,1)S(1)}, bf16[128,12,128]{0,2,1:T(8,128)(2,1)}, u32[]{:S(2)}) copy-start(bf16[128,12,128]{0,2,1:T(8,128)(2,1)} %copy-done.7) | copy-start | bytes 1179652
  118.1 21.7 %copy-start.6 = (bf16[128,12,128]{0,2,1:T(8,128)(2,1)S(1)}, bf16[128,12,128]{0,2,1:T(8,128)(2,1)}, u32[]{:S(2)}) copy-start(bf16[128,12,128]{0,2,1:T(8,128)(2,1)} %copy-done.5) | copy-start | bytes 1179652
  118.1 38.9 %all-to-all-start.1 = ((f32[16,1,4608]{2,1,0:T(1,128)}), f32[16,1,4608]{2,1,0:T(1,128)S(1)}, u32[]{:S(2)}, u32[]{:S(2)}) async-start(f32[16,1,4608]{2,1,0:T(1,128)} %bitcast.27), calls=%async_computation.2 | async-start | bytes 589824 | tf_op jit(solution)/shard_map/all_to_all | solution.py:21
  139.7 1.0 copy-start.10
Sparse Core Ops, SparseCore 0:
  74.7 60.8 reduce-scatter.1

commit v2 on v1

--- a/solution.py
+++ b/solution.py
@@ -6,6 +6,8 @@
 
 DP_SPLIT = (("z", 16), ("yh", 4), ("c", 2))
 DP = tuple(name for name, _ in DP_SPLIT)
+FSDP_SPLIT = (("yl", 2), ("x", 4))
+FSDP = tuple(name for name, _ in FSDP_SPLIT)
 
 
 def reduce_over_dp(terms):
@@ -29,7 +31,9 @@
         weight_blocks.shape[1],
         weight_blocks.shape[3],
     )
-    whole = lax.all_gather(tokens, "fsdp", axis=1, tiled=True)
+    pair = lax.all_gather(tokens, "yl", axis=0, tiled=False)
+    ring = lax.all_gather(pair, "x", axis=1, tiled=False)
+    whole = ring.transpose(2, 0, 1, 3).reshape(count_rows, -1)
     width = whole.shape[1]
     row_blocks = width // block_size
     whole_rows = whole.reshape(count_rows, row_blocks, block_size)
@@ -64,7 +68,7 @@
         )
     projected = projected_sum.astype(jnp.bfloat16).reshape(count_rows, columns * block_size)
     partial_grads = partial_grads.reshape(count_rows, width)
-    grad_tokens = lax.psum_scatter(partial_grads, "fsdp", scatter_dimension=1, tiled=True).astype(
+    grad_tokens = lax.psum_scatter(partial_grads, FSDP, scatter_dimension=1, tiled=True).astype(
         jnp.bfloat16
     )
     scale_factor = 1.0 / jnp.sqrt(jnp.float32(count_rows * lax.axis_size(DP)))
@@ -75,14 +79,14 @@
 
 def solution(mesh):
     split = Mesh(
-        mesh.devices.reshape(tuple(size for _, size in DP_SPLIT) + (mesh.shape["fsdp"],)),
-        DP + ("fsdp",),
+        mesh.devices.reshape(tuple(size for _, size in DP_SPLIT + FSDP_SPLIT)),
+        DP + FSDP,
     )
-    placed = (P(DP, "fsdp"), P("fsdp", None, None, None), P("fsdp", None), P(DP, "fsdp"))
+    placed = (P(DP, FSDP), P(FSDP, None, None, None), P(FSDP, None), P(DP, FSDP))
     return jax.shard_map(
         on_device,
         mesh=split,
         in_specs=placed,
-        out_specs=(P(DP, "fsdp"), P(DP, "fsdp"), P("fsdp", None, DP)),
+        out_specs=(P(DP, FSDP), P(DP, FSDP), P(FSDP, None, DP)),
         check_vma=False,
     )

time: 166 us -> 155 us (0.934)
  blocking collectives: 75 us -> 68.3 us
  starting transfers between devices: 23.4 us -> 19.8 us
    all_gather x1 -> x2, blocking collectives: 36.7 us -> 28.7 us  [the longest x1 23.2 us: on_device(): ring = lax.all_gather(pair, 'x', axis=1, tiled=False)]
    all_to_all x1, starting transfers between devices: 21.3 us -> 17.7 us  [reduce_over_dp(): along = lax.all_to_all(across.reshape(planes, width), 'z', 0, 0, tiled=True)]
    unnamed x27 -> x30, local copies, waits for them, and re-layouts: 6.2 us -> 5.52 us
  transfers between devices with their start and end apart: 3 -> 3, of which waited for: 1 -> 1; matrix products, arithmetic and copies ran while one was open for 12% -> 13% of each run, Pallas kernels for 0% -> 0%
where the time goes in v2:
time: 155 us; the launch traced here: 154 us
  blocking collectives  68.3 us (44%)
  local copies, waits for them, and re-layouts  24.7 us (16%)
  starting transfers between devices  19.8 us (13%)
  between operations  14.3 us (9%)
  waiting for transfers between devices  13.6 us (9%)
  matrix products  7.67 us (5%)
  other arithmetic  5.55 us (4%)
    all_to_all x1, blocking collectives, reduce_over_dp(): across = jnp.sum(lax.all_to_all(across, 'yh', 0, 0, tiled=True), axis=0)  39.6 us
    all_gather x1, blocking collectives, on_device(): ring = lax.all_gather(pair, 'x', axis=1, tiled=False)  23.2 us
    all_to_all x1, starting transfers between devices, reduce_over_dp(): along = lax.all_to_all(across.reshape(planes, width), 'z', 0, 0, tiled=True)  17.7 us
    all_to_all x1, waiting for transfers between devices, reduce_over_dp(): along = lax.all_to_all(across.reshape(planes, width), 'z', 0, 0, tiled=True)  13.6 us
    unnamed x30, local copies, waits for them, and re-layouts  5.52 us
    all_gather x1, blocking collectives, on_device(): pair = lax.all_gather(tokens, 'yl', axis=0, tiled=False)  5.5 us
    transpose x3, local copies, waits for them, and re-layouts, on_device(): jnp.einsum('tco,cbo->tcb', grad_cols, weight_slot, preferred_element_type...  5.28 us
    dynamic_slice x1, local copies, waits for them, and re-layouts, reduce_over_dp(): keep = lax.dynamic_index_in_dim(pairs, mine, axis=1, keepdims=False)  4.8 us
  transfers between devices with their start and end apart: 3, of which 1 were waited for; matrix products, arithmetic and copies ran while one was open for 13% of the time, Pallas kernels for 0%

profile of v2, /device:TPU:6, one launch (start us, length us, event | category | flops | bytes accessed | tf_op | source)
XLA Modules:
  0.0 154.0 jit_solution(8872326690080125849)
XLA Ops:
  7.2 5.5 %all-gather = bf16[256,384]{1,0:T(8,128)(2,1)S(1)} all-gather(bf16[128,384]{1,0:T(8,128)(2,1)} %param.4), channel_id=2, replica_groups=mesh['z'=16,'yh'=4,'c'=2,'yl'=2,'x'=4] {'yl'}, dimensions={0}, use_global_device_ids=true | all-gather | bytes 294912 | tf_op jit(solution)/shard_map/all_gather | solution.py:34
  12.7 23.2 %all-gather.1 = bf16[2,512,384]{2,1,0:T(8,128)(2,1)S(1)} all-gather(bf16[2,128,384]{2,1,0:T(8,128)(2,1)S(1)} %bitcast.114), channel_id=3, replica_groups=mesh['z'=16,'yh'=4,'c'=2,'yl'=2,'x'=4] {'x'}, dimensions={1}, use_global_device_ids=true | all-gather | bytes 983040 | tf_op jit(solution)/shard_map/all_gather | solution.py:35
  35.9 0.6 copy.113
  37.2 0.4 copy.130
  38.0 0.4 copy.132
  39.1 0.4 copy-done.11
  39.7 0.4 convolution_bitcast_fusion
  40.2 0.4 convolution_bitcast_fusion.1
  40.6 0.4 convolution_bitcast_fusion.2
  41.3 1.6 %copy.136 = f32[128,12,3,128]{3,2,1,0:T(4,128)S(1)} copy(f32[128,12,3,128]{3,0,1,2:T(8,128)S(1)} %pad_maximum_fusion) | data formatting | bytes 4718592 | tf_op jit(solution)/shard_map/stack | solution.py:75
  42.9 3.3 %reshape_reshape.7 = f32[64,2,4608]{2,1,0:T(2,128)} reshape(f32[128,12,3,128]{3,2,1,0:T(4,128)S(1)} %copy.136) | data formatting | bytes 4718592 | tf_op jit(solution)/shard_map/reshape;reshape | solution.py:15
  46.2 4.8 %constant_dynamic-slice_fusion.1 = (f32[64,1,4608]{2,1,0:T(1,128)S(1)}, f32[64,1,4608]{2,1,0:T(1,128)S(1)}) fusion(f32[64,2,4608]{2,1,0:T(2,128)} %reshape_reshape.7, s32[]{:T(128)S(6)} %select_n.7, s32[]{:T(128)S(6)} %select_n.8), kind=kLoop, calls=%fused_computation.49 | loop fusion | bytes 4718600 | tf_op jit(solution)/shard_map/jit(dynamic_index_in_dim)/dynamic_slice | solution.py:17
  51.0 1.1 copy.160
  52.1 2.1 %collective-permute-start = (f32[64,4608]{1,0:T(8,128)}, f32[64,4608]{1,0:T(8,128)}, u32[]{:S(2)}, u32[]{:S(2)}) collective-permute-start(f32[64,4608]{1,0:T(8,128)} %bitcast.102), channel_id=1, source_target_pairs={{0,8},{8,0},{1,9},{9,1},{2,10},{10,2},{3,11},{11,3},{4,12},{12,4},... | collective-permute-start | bytes 3538952 | tf_op jit(solution)/shard_map/ppermute | solution.py:19
  54.2 1.2 convolution_bitcast_fusion.5
  55.6 2.5 %copy.123 = f32[128,12,128]{2,1,0:T(8,128)} copy(f32[128,12,128]{0,2,1:T(8,128)} %convolution_bitcast_fusion.5) | data formatting | bytes 1572864 | tf_op jit(solution)/shard_map/tco,cbo->tcb/transpose | solution.py:57
  58.2 1.4 copy.126
  59.8 1.4 copy.129
  61.2 0.9 fusion.18
  62.4 0.9 fusion.22
  63.6 1.0 add_add_fusion
  64.7 1.4 copy.159
  66.1 1.4 bitcast_add_fusion
  67.9 1.2 copy.137
  69.1 39.6 %all_to_all.18 = f32[4,1,73728]{2,1,0:T(1,128)S(1)} all-to-all(f32[4,1,73728]{2,1,0:T(1,128)S(1)} %copy.137), channel_id=1, replica_groups=mesh['z'=16,'yh'=4,'c'=2,'yl'=2,'x'=4] {'yh'}, dimensions={0} | all-to-all | bytes 2359296 | tf_op jit(solution)/shard_map/all_to_all | solution.py:22
  108.7 2.1 %reduce_sum.18 = f32[73728]{0:T(1024)} reduce(f32[4,1,73728]{2,1,0:T(1,128)S(1)} %all_to_all.18, f32[]{:T(128)} %constant.20.clone.1), dimensions={0,1}, to_apply=%region_1.2 | reduce | flops 221184 | bytes 1474564 | tf_op jit(solution)/shard_map/reduce_sum | solution.py:22
  110.8 17.7 %all-to-all-start.1 = ((f32[16,1,4608]{2,1,0:T(1,128)}), f32[16,1,4608]{2,1,0:T(1,128)S(1)}, u32[]{:S(2)}, u32[]{:S(2)}) async-start(f32[16,1,4608]{2,1,0:T(1,128)} %bitcast.30), calls=%async_computation.2 | async-start | bytes 589824 | tf_op jit(solution)/shard_map/all_to_all | solution.py:23
  129.2 0.7 copy-done.10
  130.2 0.9 copy.139
  131.1 1.6 %convert_element_type.41 = bf16[128,384]{1,0:T(8,128)(2,1)} convert(f32[128,384]{1,0:T(8,128)} %reduce-scatter.2.cloned.1.call-done) | non-fusion elementwise | flops 49152 | bytes 294912 | tf_op jit(solution)/shard_map/convert_element_type | solution.py:71
  132.7 13.6 %all-to-all-done.1 = f32[16,1,4608]{2,1,0:T(1,128)S(1)} async-done(((f32[16,1,4608]{2,1,0:T(1,128)}), f32[16,1,4608]{2,1,0:T(1,128)S(1)}, u32[]{:S(2)}, u32[]{:S(2)}) %all-to-all-start.1) | async-done | bytes 294944 | tf_op jit(solution)/shard_map/all_to_all | solution.py:23
  146.5 0.6 mul.11
  (44 shorter events, 5.0 us)
Async XLA Ops:
  7.2 124.0 %reduce-scatter.2.cloned.1.call-start = ((), (), s32[]{:S(2)}) async-start(), calls=%async_computation.3 | async-start | bytes 1769472 | tf_op jit(solution)/shard_map/reduce_scatter | solution.py:71
  35.9 0.9 copy-start.12
  37.6 3.0 %copy-start.7 = (bf16[128,12,128]{0,2,1:T(8,128)(2,1)}, bf16[128,12,128]{0,2,1:T(8,128)(2,1)S(1)}, u32[]{:S(2)}) copy-start(bf16[128,12,128]{0,2,1:T(8,128)(2,1)S(1)} %copy.130) | copy-start | bytes 1179652
  38.3 1.8 %copy-start.5 = (bf16[128,12,128]{0,2,1:T(8,128)(2,1)}, bf16[128,12,128]{0,2,1:T(8,128)(2,1)S(1)}, u32[]{:S(2)}) copy-start(bf16[128,12,128]{0,2,1:T(8,128)(2,1)S(1)} %copy.132) | copy-start | bytes 1179652
  38.4 1.1 copy-start.11
  39.5 0.7 copy-start.9
  51.0 3.2 %copy-start = (bf16[12,3,128,128]{3,2,1,0:T(8,128)(2,1)S(1)}, bf16[12,3,128,128]{3,2,1,0:T(8,128)(2,1)}, u32[]{:S(2)}) copy-start(bf16[12,3,128,128]{3,2,1,0:T(8,128)(2,1)} %param.5) | copy-start | bytes 3538948
  52.1 14.0 %collective-permute-start = (f32[64,4608]{1,0:T(8,128)}, f32[64,4608]{1,0:T(8,128)}, u32[]{:S(2)}, u32[]{:S(2)}) collective-permute-start(f32[64,4608]{1,0:T(8,128)} %bitcast.102), channel_id=1, source_target_pairs={{0,8},{8,0},{1,9},{9,1},{2,10},{10,2},{3,11},{11,3},{4,12},{12,4},... | collective-permute-start | bytes 3538952 | tf_op jit(solution)/shard_map/ppermute | solution.py:19
  59.8 1.4 copy-start.3
  61.2 1.2 copy-start.2
  62.4 1.2 copy-start.4
  108.7 19.9 %copy-start.1 = (bf16[12,3,128,128]{3,2,1,0:T(8,128)(2,1)S(1)}, bf16[12,3,128,128]{3,2,1,0:T(8,128)(2,1)}, u32[]{:S(2)}) copy-start(bf16[12,3,128,128]{3,2,1,0:T(8,128)(2,1)} %param.5) | copy-start | bytes 3538948
  108.7 19.9 %copy-start.8 = (bf16[128,12,128]{0,2,1:T(8,128)(2,1)S(1)}, bf16[128,12,128]{0,2,1:T(8,128)(2,1)}, u32[]{:S(2)}) copy-start(bf16[128,12,128]{0,2,1:T(8,128)(2,1)} %copy-done.7) | copy-start | bytes 1179652
  110.8 18.1 %copy-start.6 = (bf16[128,12,128]{0,2,1:T(8,128)(2,1)S(1)}, bf16[128,12,128]{0,2,1:T(8,128)(2,1)}, u32[]{:S(2)}) copy-start(bf16[128,12,128]{0,2,1:T(8,128)(2,1)} %copy-done.5) | copy-start | bytes 1179652
  110.8 35.5 %all-to-all-start.1 = ((f32[16,1,4608]{2,1,0:T(1,128)}), f32[16,1,4608]{2,1,0:T(1,128)S(1)}, u32[]{:S(2)}, u32[]{:S(2)}) async-start(f32[16,1,4608]{2,1,0:T(1,128)} %bitcast.30), calls=%async_computation.2 | async-start | bytes 589824 | tf_op jit(solution)/shard_map/all_to_all | solution.py:23
  128.9 1.0 copy-start.10
Sparse Core Ops, SparseCore 0:
  66.2 58.7 reduce-scatter.1

commit v3 on v2

--- a/solution.py
+++ b/solution.py
@@ -10,12 +10,8 @@
 FSDP = tuple(name for name, _ in FSDP_SPLIT)
 
 
-def reduce_over_dp(terms):
-    rows, width = terms.shape
-    pairs = terms.reshape(rows // 2, 2, width)
-    mine = lax.axis_index("c")
-    keep = lax.dynamic_index_in_dim(pairs, mine, axis=1, keepdims=False)
-    send = lax.dynamic_index_in_dim(pairs, 1 - mine, axis=1, keepdims=False)
+def reduce_over_dp(keep, send):
+    rows, width = keep.shape
     halved = keep + lax.ppermute(send, "c", [(0, 1), (1, 0)])
     planes, lanes = DP_SPLIT[0][1], DP_SPLIT[1][1]
     across = halved.reshape(planes, lanes, width).transpose(1, 0, 2).reshape(lanes, planes * width)
@@ -41,7 +37,8 @@
     row_ids = jnp.arange(row_blocks, dtype=jnp.int32)
     projected_sum = jnp.zeros((count_rows, columns, block_size), jnp.float32)
     partial_grads = jnp.zeros((count_rows, row_blocks, block_size), jnp.float32)
-    slot_terms = []
+    keep_terms, send_terms = [], []
+    first_core = lax.axis_index("c") == 0
     for slot in range(slots):
         selector = row_ids[:, None] == pattern[:, slot][None, :]
         picked_slot = jnp.einsum(
@@ -63,17 +60,20 @@
             selector.astype(jnp.float32),
             precision=lax.Precision.HIGHEST,
         )
-        slot_terms.append(
-            jnp.einsum("tcb,tco->bco", picked_slot, grad_cols, preferred_element_type=jnp.float32)
-        )
+        even, odd = picked_slot[:, :, 0::2], picked_slot[:, :, 1::2]
+        for terms, rows in ((keep_terms, jnp.where(first_core, even, odd)), (send_terms, jnp.where(first_core, odd, even))):
+            terms.append(
+                jnp.einsum("tcb,tco->bco", rows, grad_cols, preferred_element_type=jnp.float32)
+            )
     projected = projected_sum.astype(jnp.bfloat16).reshape(count_rows, columns * block_size)
     partial_grads = partial_grads.reshape(count_rows, width)
     grad_tokens = lax.psum_scatter(partial_grads, FSDP, scatter_dimension=1, tiled=True).astype(
         jnp.bfloat16
     )
     scale_factor = 1.0 / jnp.sqrt(jnp.float32(count_rows * lax.axis_size(DP)))
-    weight_terms = jnp.stack(slot_terms, axis=2).reshape(block_size, columns * slots * block_size)
-    grad_weight = reduce_over_dp(weight_terms).reshape(columns, slots, block_size) * scale_factor
+    keep = jnp.stack(keep_terms, axis=2).reshape(block_size // 2, columns * slots * block_size)
+    send = jnp.stack(send_terms, axis=2).reshape(block_size // 2, columns * slots * block_size)
+    grad_weight = reduce_over_dp(keep, send).reshape(columns, slots, block_size) * scale_factor
     return (projected, grad_tokens, grad_weight)
 
 

time: 155 us -> 224 us (1.45)
  local copies, waits for them, and re-layouts: 24.7 us -> 79 us
  blocking collectives: 68.3 us -> 75.6 us
  matrix products: 7.67 us -> 14.1 us
  starting transfers between devices: 19.8 us -> 16.1 us
  other arithmetic: 5.55 us -> 9.19 us
    slice x0 -> x6, local copies, waits for them, and re-layouts: none -> 55.1 us  [on_device(): even, odd = (picked_slot[:, :, 0::2], picked_slot[:, :, 1::2])]
    all_to_all x1, blocking collectives: 39.6 us -> 46.9 us  [reduce_over_dp(): across = jnp.sum(lax.all_to_all(across, 'yh', 0, 0, tiled=True), axis=0)]
    dynamic_slice x1 -> x0, local copies, waits for them, and re-layouts: 4.8 us -> none  [reduce_over_dp(): keep = lax.dynamic_index_in_dim(pairs, mine, axis=1, keepdims=False)]
    all_to_all x1, starting transfers between devices: 17.7 us -> 13.8 us  [reduce_over_dp(): along = lax.all_to_all(across.reshape(planes, width), 'z', 0, 0, tiled=True)]
    select_n x0 -> x2, other arithmetic: none -> 3.38 us  [on_device(): jnp.where(first_core, odd, even)]
    another operation x2, local copies, waits for them, and re-layouts: 4.89 us -> 1.62 us  [the longest x1 0.81 us: on_device(): jnp.stack(send_terms, axis=2)]
    reshape x0 -> x2, local copies, waits for them, and re-layouts: none -> 3 us  [the longest x1 1.5 us: on_device(): jnp.stack(keep_terms, axis=2)]
    dot_general x3, matrix products: 1.66 us -> 4.44 us  [on_device(): jnp.einsum('tco,cbo->tcb', grad_cols, weight_slot, preferred_element_type...]
  transfers between devices with their start and end apart: 3 -> 3, of which waited for: 1 -> 1; matrix products, arithmetic and copies ran while one was open for 13% -> 14% of each run, Pallas kernels for 0% -> 0%
where the time goes in v3:
time: 224 us; the launch traced here: 223 us
  local copies, waits for them, and re-layouts  79 us (35%)
  blocking collectives  75.6 us (34%)
  starting transfers between devices  16.1 us (7%)
  waiting for transfers between devices  15 us (7%)
  between operations  14.2 us (6%)
  matrix products  14.1 us (6%)
  other arithmetic  9.19 us (4%)
    slice x6, local copies, waits for them, and re-layouts, on_device(): even, odd = (picked_slot[:, :, 0::2], picked_slot[:, :, 1::2])  55.1 us
    all_to_all x1, blocking collectives, reduce_over_dp(): across = jnp.sum(lax.all_to_all(across, 'yh', 0, 0, tiled=True), axis=0)  46.9 us
    all_gather x1, blocking collectives, on_device(): ring = lax.all_gather(pair, 'x', axis=1, tiled=False)  23.2 us
    all_to_all x1, waiting for transfers between devices, reduce_over_dp(): along = lax.all_to_all(across.reshape(planes, width), 'z', 0, 0, tiled=True)  14.9 us
    all_to_all x1, starting transfers between devices, reduce_over_dp(): along = lax.all_to_all(across.reshape(planes, width), 'z', 0, 0, tiled=True)  13.8 us
    transpose x3, local copies, waits for them, and re-layouts, on_device(): jnp.einsum('tco,cbo->tcb', grad_cols, weight_slot, preferred_element_type...  5.77 us
    unnamed x17, local copies, waits for them, and re-layouts  5.68 us
    all_gather x1, blocking collectives, on_device(): pair = lax.all_gather(tokens, 'yl', axis=0, tiled=False)  5.48 us
  transfers between devices with their start and end apart: 3, of which 1 were waited for; matrix products, arithmetic and copies ran while one was open for 14% of the time, Pallas kernels for 0%

profile of v3, /device:TPU:6, one launch (start us, length us, event | category | flops | bytes accessed | tf_op | source)
XLA Modules:
  0.0 223.2 jit_solution(5032836821537328556)
XLA Ops:
  8.0 5.5 %all-gather = bf16[256,384]{1,0:T(8,128)(2,1)S(1)} all-gather(bf16[128,384]{1,0:T(8,128)(2,1)} %param.4), channel_id=2, replica_groups=mesh['z'=16,'yh'=4,'c'=2,'yl'=2,'x'=4] {'yl'}, dimensions={0}, use_global_device_ids=true | all-gather | bytes 294912 | tf_op jit(solution)/shard_map/all_gather | solution.py:30
  13.5 23.2 %all-gather.1 = bf16[2,512,384]{2,1,0:T(8,128)(2,1)S(1)} all-gather(bf16[2,128,384]{2,1,0:T(8,128)(2,1)S(1)} %bitcast.121), channel_id=3, replica_groups=mesh['z'=16,'yh'=4,'c'=2,'yl'=2,'x'=4] {'x'}, dimensions={1}, use_global_device_ids=true | all-gather | bytes 983040 | tf_op jit(solution)/shard_map/all_gather | solution.py:31
  38.0 9.0 %slice.44 = bf16[128,12,64]{2,1,0:T(8,128)(2,1)S(1)} slice(bf16[128,12,128]{2,1,0:T(8,128)(2,1)S(1)} %fusion.2), slice={[0:128:1], [0:12:1], [0:128:2]} | slice | bytes 393216 | tf_op jit(solution)/shard_map/slice | solution.py:63
  46.9 9.4 %slice.45 = bf16[128,12,64]{2,1,0:T(8,128)(2,1)} slice(bf16[128,12,128]{2,1,0:T(8,128)(2,1)S(1)} %fusion.2), slice={[0:128:1], [0:12:1], [1:128:2]} | slice | bytes 393216 | tf_op jit(solution)/shard_map/slice | solution.py:63
  56.7 9.3 %slice.46 = bf16[128,12,64]{2,1,0:T(8,128)(2,1)} slice(bf16[128,12,128]{2,1,0:T(8,128)(2,1)S(1)} %fusion.3), slice={[0:128:1], [0:12:1], [0:128:2]} | slice | bytes 393216 | tf_op jit(solution)/shard_map/slice | solution.py:63
  66.0 9.4 %slice.47 = bf16[128,12,64]{2,1,0:T(8,128)(2,1)} slice(bf16[128,12,128]{2,1,0:T(8,128)(2,1)S(1)} %fusion.3), slice={[0:128:1], [0:12:1], [1:128:2]} | slice | bytes 393216 | tf_op jit(solution)/shard_map/slice | solution.py:63
  75.8 9.0 %slice.42 = bf16[128,12,64]{2,1,0:T(8,128)(2,1)S(1)} slice(bf16[128,12,128]{2,1,0:T(8,128)(2,1)S(1)} %fusion.1), slice={[0:128:1], [0:12:1], [0:128:2]} | slice | bytes 393216 | tf_op jit(solution)/shard_map/slice | solution.py:63
  84.7 9.1 %slice.43 = bf16[128,12,64]{2,1,0:T(8,128)(2,1)S(1)} slice(bf16[128,12,128]{2,1,0:T(8,128)(2,1)S(1)} %fusion.1), slice={[0:128:1], [0:12:1], [1:128:2]} | slice | bytes 393216 | tf_op jit(solution)/shard_map/slice | solution.py:63
  93.8 1.2 copy.125
  95.0 2.5 %broadcast_select_fusion = (bf16[128,12,64]{2,1,0:T(8,128)(2,1)S(1)}, bf16[128,12,64]{2,1,0:T(8,128)(2,1)}, bf16[128,12,64]{2,1,0:T(8,128)(2,1)}, bf16[128,12,64]{2,1,0:T(8,128)(2,1)S(1)}) fusion(bf16[128,12,64]{2,1,0:T(8,128)(2,1)} %slice.47, bf16[128,12,64]{2,1,0:T(8,128)(2,1)} %slice.46, pred[]{:T(512)S(6)} %eq.60, bf16[128,12,64]{2,1,0:T(8,128)(2,1)S(1)} %slice.44, ...), kind=kLoop, calls=%fused_computation.23 | loop fusion | flops 393216 | bytes 1572865 | tf_op jit(solution)/shard_map/jit(_where)/select_n | solution.py:64
  100.5 1.5 reshape.42
  102.0 2.2 collective-permute-start
  104.2 2.1 convolution_bitcast_fusion.2
  106.4 1.2 convolution_bitcast_fusion.1
  107.5 1.1 convolution_bitcast_fusion
  108.7 1.6 copy.128
  110.3 2.0 fusion.27
  112.4 1.6 copy.131
  114.0 2.5 %copy.134 = f32[128,12,128]{2,1,0:T(8,128)} copy(f32[128,12,128]{0,2,1:T(8,128)} %convolution_bitcast_fusion) | data formatting | bytes 1572864 | tf_op jit(solution)/shard_map/tco,cbo->tcb/transpose | solution.py:54
  118.2 1.0 add_add_fusion
  119.2 1.4 copy.190
  124.1 1.5 reshape.41
  125.6 1.7 add.28
  127.3 1.4 reshape.43
  128.7 1.7 copy.191
  130.4 2.5 %all_to_all.16 = f32[4,1,73728]{2,1,0:T(1,128)} reshape(f32[4,16,4608]{2,1,0:T(8,128)S(1)} %bitcast.118) | data formatting | bytes 2359296 | tf_op jit(solution)/shard_map/all_to_all | solution.py:18
  132.9 46.9 %all_to_all.19 = f32[4,1,73728]{2,1,0:T(1,128)S(1)} all-to-all(f32[4,1,73728]{2,1,0:T(1,128)} %all_to_all.16), channel_id=1, replica_groups=mesh['z'=16,'yh'=4,'c'=2,'yl'=2,'x'=4] {'yh'}, dimensions={0} | all-to-all | bytes 2359296 | tf_op jit(solution)/shard_map/all_to_all | solution.py:18
  179.8 2.1 reduce_sum.18
  181.9 13.8 %all-to-all-start.1 = ((f32[16,1,4608]{2,1,0:T(1,128)}), f32[16,1,4608]{2,1,0:T(1,128)S(1)}, u32[]{:S(2)}, u32[]{:S(2)}) async-start(f32[16,1,4608]{2,1,0:T(1,128)} %bitcast.35), calls=%async_computation.2 | async-start | bytes 589824 | tf_op jit(solution)/shard_map/all_to_all | solution.py:19
  195.7 1.4 fusion.9
  199.0 1.6 convert_element_type.41
  200.6 14.9 %all-to-all-done.1 = f32[16,1,4608]{2,1,0:T(1,128)S(1)} async-done(((f32[16,1,4608]{2,1,0:T(1,128)}), f32[16,1,4608]{2,1,0:T(1,128)S(1)}, u32[]{:S(2)}, u32[]{:S(2)}) %all-to-all-start.1) | async-done | bytes 294944 | tf_op jit(solution)/shard_map/all_to_all | solution.py:19
  (42 shorter events, 13.4 us)
Async XLA Ops:
  7.2 191.8 %reduce-scatter.2.cloned.1.call-start = ((), (), s32[]{:S(2)}) async-start(), calls=%async_computation.3 | async-start | bytes 1769472 | tf_op jit(solution)/shard_map/reduce_scatter | solution.py:70
  102.0 4.4 %copy-start.1 = (bf16[12,3,128,128]{3,2,1,0:T(8,128)(2,1)S(1)}, bf16[12,3,128,128]{3,2,1,0:T(8,128)(2,1)}, u32[]{:S(2)}) copy-start(bf16[12,3,128,128]{3,2,1,0:T(8,128)(2,1)} %param.5) | copy-start | bytes 3538948
  102.0 23.6 %collective-permute-start = (f32[64,4608]{1,0:T(8,128)}, f32[64,4608]{1,0:T(8,128)}, u32[]{:S(2)}, u32[]{:S(2)}) collective-permute-start(f32[64,4608]{1,0:T(8,128)} %reshape.42), channel_id=1, source_target_pairs={{0,8},{8,0},{1,9},{9,1},{2,10},{10,2},{3,11},{11,3},{4,12},{12,4},... | collective-permute-start | bytes 3538952 | tf_op jit(solution)/shard_map/ppermute | solution.py:15
  116.5 1.4 copy-start
  116.5 1.7 copy-start.3
  120.7 1.0 copy-start.5
  120.7 1.4 copy-start.4
  121.7 1.1 copy-start.6
  181.9 15.3 %copy-start.2 = (bf16[12,3,128,128]{3,2,1,0:T(8,128)(2,1)S(1)}, bf16[12,3,128,128]{3,2,1,0:T(8,128)(2,1)}, u32[]{:S(2)}) copy-start(bf16[12,3,128,128]{3,2,1,0:T(8,128)(2,1)} %param.5) | copy-start | bytes 3538948
  181.9 33.6 %all-to-all-start.1 = ((f32[16,1,4608]{2,1,0:T(1,128)}), f32[16,1,4608]{2,1,0:T(1,128)S(1)}, u32[]{:S(2)}, u32[]{:S(2)}) async-start(f32[16,1,4608]{2,1,0:T(1,128)} %bitcast.35), calls=%async_computation.2 | async-start | bytes 589824 | tf_op jit(solution)/shard_map/all_to_all | solution.py:19
Sparse Core Ops, SparseCore 0:
  120.8 61.6 reduce-scatter.1

commit v4 on v3

--- a/solution.py
+++ b/solution.py
@@ -38,7 +38,11 @@
     projected_sum = jnp.zeros((count_rows, columns, block_size), jnp.float32)
     partial_grads = jnp.zeros((count_rows, row_blocks, block_size), jnp.float32)
     keep_terms, send_terms = [], []
-    first_core = lax.axis_index("c") == 0
+    core = lax.axis_index("c")
+    column_ids = jnp.arange(block_size, dtype=jnp.int32)[:, None]
+    pair_ids = 2 * jnp.arange(block_size // 2, dtype=jnp.int32)[None, :]
+    keep_cols = (column_ids == pair_ids + core).astype(jnp.bfloat16)
+    send_cols = (column_ids == pair_ids + 1 - core).astype(jnp.bfloat16)
     for slot in range(slots):
         selector = row_ids[:, None] == pattern[:, slot][None, :]
         picked_slot = jnp.einsum(
@@ -60,8 +64,10 @@
             selector.astype(jnp.float32),
             precision=lax.Precision.HIGHEST,
         )
-        even, odd = picked_slot[:, :, 0::2], picked_slot[:, :, 1::2]
-        for terms, rows in ((keep_terms, jnp.where(first_core, even, odd)), (send_terms, jnp.where(first_core, odd, even))):
+        for terms, cols in ((keep_terms, keep_cols), (send_terms, send_cols)):
+            rows = jnp.einsum(
+                "tcb,bm->tcm", picked_slot, cols, preferred_element_type=jnp.float32
+            ).astype(jnp.bfloat16)
             terms.append(
                 jnp.einsum("tcb,tco->bco", rows, grad_cols, preferred_element_type=jnp.float32)
             )

time: 224 us -> 167 us (0.75)
  local copies, waits for them, and re-layouts: 79 us -> 22.9 us
  other arithmetic: 9.19 us -> 5.88 us
    slice x6 -> x0, local copies, waits for them, and re-layouts: 55.1 us -> none  [on_device(): even, odd = (picked_slot[:, :, 0::2], picked_slot[:, :, 1::2])]
    select_n x2 -> x0, other arithmetic: 3.38 us -> none  [on_device(): jnp.where(first_core, odd, even)]
    unnamed x17 -> x11, local copies, waits for them, and re-layouts: 5.68 us -> 3.6 us
  transfers between devices with their start and end apart: 3 -> 3, of which waited for: 1 -> 1; matrix products, arithmetic and copies ran while one was open for 14% -> 20% of each run, Pallas kernels for 0% -> 0%
where the time goes in v4:
time: 167 us; the launch traced here: 166 us
  blocking collectives  74.9 us (45%)
  local copies, waits for them, and re-layouts  22.9 us (14%)
  starting transfers between devices  16.8 us (10%)
  matrix products  16.2 us (10%)
  waiting for transfers between devices  14.9 us (9%)
  between operations  14.2 us (9%)
  other arithmetic  5.88 us (4%)
    all_to_all x1, blocking collectives, reduce_over_dp(): across = jnp.sum(lax.all_to_all(across, 'yh', 0, 0, tiled=True), axis=0)  46.2 us
    all_gather x1, blocking collectives, on_device(): ring = lax.all_gather(pair, 'x', axis=1, tiled=False)  23.2 us
    all_to_all x1, waiting for transfers between devices, reduce_over_dp(): along = lax.all_to_all(across.reshape(planes, width), 'z', 0, 0, tiled=True)  14.9 us
    all_to_all x1, starting transfers between devices, reduce_over_dp(): along = lax.all_to_all(across.reshape(planes, width), 'z', 0, 0, tiled=True)  14.6 us
    transpose x3, local copies, waits for them, and re-layouts, on_device(): jnp.einsum('tco,cbo->tcb', grad_cols, weight_slot, preferred_element_type...  6.37 us
    all_gather x1, blocking collectives, on_device(): pair = lax.all_gather(tokens, 'yl', axis=0, tiled=False)  5.48 us
    dot_general x3, matrix products, on_device(): jnp.einsum('tcb,rc->trb', backward_slot, selector.astype(jnp.float32), pr...  5.4 us
    unnamed x11, local copies, waits for them, and re-layouts  3.6 us
  transfers between devices with their start and end apart: 3, of which 1 were waited for; matrix products, arithmetic and copies ran while one was open for 20% of the time, Pallas kernels for 0%

profile of v4, /device:TPU:6, one launch (start us, length us, event | category | flops | bytes accessed | tf_op | source)
XLA Modules:
  0.0 165.8 jit_solution(9926956294661141362)
XLA Ops:
  7.2 1.2 copy.113
  8.4 1.3 slice_bitcast_fusion
  9.7 5.5 %all-gather = bf16[256,384]{1,0:T(8,128)(2,1)S(1)} all-gather(bf16[128,384]{1,0:T(8,128)(2,1)} %param.4), channel_id=2, replica_groups=mesh['z'=16,'yh'=4,'c'=2,'yl'=2,'x'=4] {'yl'}, dimensions={0}, use_global_device_ids=true | all-gather | bytes 294912 | tf_op jit(solution)/shard_map/all_gather | solution.py:30
  15.2 23.2 %all-gather.1 = bf16[2,512,384]{2,1,0:T(8,128)(2,1)S(1)} all-gather(bf16[2,128,384]{2,1,0:T(8,128)(2,1)S(1)} %bitcast.137), channel_id=3, replica_groups=mesh['z'=16,'yh'=4,'c'=2,'yl'=2,'x'=4] {'x'}, dimensions={1}, use_global_device_ids=true | all-gather | bytes 983040 | tf_op jit(solution)/shard_map/all_gather | solution.py:31
  41.1 1.0 fusion.1
  42.8 0.8 copy.136
  43.6 1.5 reshape.54
  45.1 2.2 %collective-permute-start = (f32[64,4608]{1,0:T(8,128)}, f32[64,4608]{1,0:T(8,128)}, u32[]{:S(2)}, u32[]{:S(2)}) collective-permute-start(f32[64,4608]{1,0:T(8,128)} %reshape.54), channel_id=1, source_target_pairs={{0,8},{8,0},{1,9},{9,1},{2,10},{10,2},{3,11},{11,3},{4,12},{12,4},... | collective-permute-start | bytes 3538952 | tf_op jit(solution)/shard_map/ppermute | solution.py:15
  47.4 1.3 convolution_bitcast_fusion.2
  48.6 1.1 convolution_bitcast_fusion.1
  49.8 1.2 convolution_bitcast_fusion
  50.9 1.4 copy.116
  52.3 2.1 %fusion.59 = f32[24,128,128]{2,0,1:T(8,128)S(1)} fusion(f32[128,12,128]{2,1,0:T(8,128)} %copy.116, s32[12]{0:T(128)S(1)} %copy-done.3), kind=kOutput, calls=%fused_computation.66 | convolution fusion | flops 56623392 | bytes 2359344 | tf_op jit(solution)/shard_map/tcb,rc->trb/dot_general | solution.py:61
  54.4 2.5 %copy.119 = f32[128,12,128]{2,1,0:T(8,128)} copy(f32[128,12,128]{0,2,1:T(8,128)} %convolution_bitcast_fusion.1) | data formatting | bytes 1572864 | tf_op jit(solution)/shard_map/tco,cbo->tcb/transpose | solution.py:58
  56.9 2.5 %copy.122 = f32[128,12,128]{2,1,0:T(8,128)} copy(f32[128,12,128]{0,2,1:T(8,128)} %convolution_bitcast_fusion) | data formatting | bytes 1572864 | tf_op jit(solution)/shard_map/tco,cbo->tcb/transpose | solution.py:58
  59.4 2.2 %fusion.63 = f32[24,128,128]{2,0,1:T(8,128)S(1)} fusion(f32[128,12,128]{2,1,0:T(8,128)} %copy.119, s32[12]{0:T(128)S(1)} %get-tuple-element.20), kind=kOutput, calls=%fused_computation.68 | convolution fusion | flops 56623392 | bytes 2359344 | tf_op jit(solution)/shard_map/tcb,rc->trb/dot_general | solution.py:61
  61.7 1.1 add_add_fusion
  62.8 1.4 copy.184
  66.0 0.8 copy.129
  66.8 1.5 reshape.53
  68.3 1.7 %add.54 = f32[64,4608]{1,0:T(8,128)S(1)} add(f32[64,4608]{1,0:T(8,128)} %reshape.53, f32[64,4608]{1,0:T(8,128)} %collective-permute-done) | non-fusion elementwise | flops 294912 | bytes 3538944 | tf_op jit(solution)/shard_map/add | solution.py:15
  70.0 1.4 reshape.55
  71.4 1.7 copy.185
  73.0 2.5 %all_to_all.16 = f32[4,1,73728]{2,1,0:T(1,128)} reshape(f32[4,16,4608]{2,1,0:T(8,128)S(1)} %bitcast.134) | data formatting | bytes 2359296 | tf_op jit(solution)/shard_map/all_to_all | solution.py:18
  75.5 46.2 %all_to_all.19 = f32[4,1,73728]{2,1,0:T(1,128)S(1)} all-to-all(f32[4,1,73728]{2,1,0:T(1,128)} %all_to_all.16), channel_id=1, replica_groups=mesh['z'=16,'yh'=4,'c'=2,'yl'=2,'x'=4] {'yh'}, dimensions={0} | all-to-all | bytes 2359296 | tf_op jit(solution)/shard_map/all_to_all | solution.py:18
  121.8 2.1 %reduce_sum.18 = f32[73728]{0:T(1024)} reduce(f32[4,1,73728]{2,1,0:T(1,128)S(1)} %all_to_all.19, f32[]{:T(128)} %constant.12.clone.1), dimensions={0,1}, to_apply=%region_1.0 | reduce | flops 221184 | bytes 1474564 | tf_op jit(solution)/shard_map/reduce_sum | solution.py:18
  123.9 14.6 %all-to-all-start.1 = ((f32[16,1,4608]{2,1,0:T(1,128)}), f32[16,1,4608]{2,1,0:T(1,128)S(1)}, u32[]{:S(2)}, u32[]{:S(2)}) async-start(f32[16,1,4608]{2,1,0:T(1,128)} %bitcast.37), calls=%async_computation.2 | async-start | bytes 589824 | tf_op jit(solution)/shard_map/all_to_all | solution.py:19
  138.5 1.4 fusion.9
  140.7 0.9 copy.140
  141.7 1.6 convert_element_type.61
  143.3 14.9 %all-to-all-done.1 = f32[16,1,4608]{2,1,0:T(1,128)S(1)} async-done(((f32[16,1,4608]{2,1,0:T(1,128)}), f32[16,1,4608]{2,1,0:T(1,128)S(1)}, u32[]{:S(2)}, u32[]{:S(2)}) %all-to-all-start.1) | async-done | bytes 294944 | tf_op jit(solution)/shard_map/all_to_all | solution.py:19
  158.4 0.6 mul.29
  (29 shorter events, 6.2 us)
Async XLA Ops:
  7.2 134.5 %reduce-scatter.2.cloned.1.call-start = ((), (), s32[]{:S(2)}) async-start(), calls=%async_computation.3 | async-start | bytes 1769472 | tf_op jit(solution)/shard_map/reduce_scatter | solution.py:76
  45.1 3.5 %copy-start = (bf16[12,3,128,128]{3,2,1,0:T(8,128)(2,1)S(1)}, bf16[12,3,128,128]{3,2,1,0:T(8,128)(2,1)}, u32[]{:S(2)}) copy-start(bf16[12,3,128,128]{3,2,1,0:T(8,128)(2,1)} %param.5) | copy-start | bytes 3538948
  45.1 23.1 %collective-permute-start = (f32[64,4608]{1,0:T(8,128)}, f32[64,4608]{1,0:T(8,128)}, u32[]{:S(2)}, u32[]{:S(2)}) collective-permute-start(f32[64,4608]{1,0:T(8,128)} %reshape.54), channel_id=1, source_target_pairs={{0,8},{8,0},{1,9},{9,1},{2,10},{10,2},{3,11},{11,3},{4,12},{12,4},... | collective-permute-start | bytes 3538952 | tf_op jit(solution)/shard_map/ppermute | solution.py:15
  50.9 1.4 copy-start.3
  59.4 2.2 %copy-start.2 = (f32[128,12,128]{2,1,0:T(8,128)S(1)}, f32[128,12,128]{2,1,0:T(8,128)}, u32[]{:S(2)}) copy-start(f32[128,12,128]{2,1,0:T(8,128)} %copy.122) | copy-start | bytes 2359300
  123.9 16.0 %copy-start.1 = (bf16[12,3,128,128]{3,2,1,0:T(8,128)(2,1)S(1)}, bf16[12,3,128,128]{3,2,1,0:T(8,128)(2,1)}, u32[]{:S(2)}) copy-start(bf16[12,3,128,128]{3,2,1,0:T(8,128)(2,1)} %param.5) | copy-start | bytes 3538948
  123.9 34.3 %all-to-all-start.1 = ((f32[16,1,4608]{2,1,0:T(1,128)}), f32[16,1,4608]{2,1,0:T(1,128)S(1)}, u32[]{:S(2)}, u32[]{:S(2)}) async-start(f32[16,1,4608]{2,1,0:T(1,128)} %bitcast.37), calls=%async_computation.2 | async-start | bytes 589824 | tf_op jit(solution)/shard_map/all_to_all | solution.py:19
Sparse Core Ops, SparseCore 0:
  64.3 61.7 reduce-scatter.1

commit v5 on v2

--- a/solution.py
+++ b/solution.py
@@ -14,8 +14,9 @@
     rows, width = terms.shape
     pairs = terms.reshape(rows // 2, 2, width)
     mine = lax.axis_index("c")
-    keep = lax.dynamic_index_in_dim(pairs, mine, axis=1, keepdims=False)
-    send = lax.dynamic_index_in_dim(pairs, 1 - mine, axis=1, keepdims=False)
+    first = mine == 0
+    keep = jnp.where(first, pairs[:, 0], pairs[:, 1])
+    send = jnp.where(first, pairs[:, 1], pairs[:, 0])
     halved = keep + lax.ppermute(send, "c", [(0, 1), (1, 0)])
     planes, lanes = DP_SPLIT[0][1], DP_SPLIT[1][1]
     across = halved.reshape(planes, lanes, width).transpose(1, 0, 2).reshape(lanes, planes * width)

time: 155 us -> 159 us (1.026)
  other arithmetic: 5.55 us -> 10.4 us
  local copies, waits for them, and re-layouts: 24.7 us -> 21.8 us
  matrix products: 7.67 us -> 9.57 us
    slice x0 -> x1, other arithmetic: none -> 4.8 us  [reduce_over_dp(): keep = jnp.where(first, pairs[:, 0], pairs[:, 1])]
    dynamic_slice x1 -> x0, local copies, waits for them, and re-layouts: 4.8 us -> none  [reduce_over_dp(): keep = lax.dynamic_index_in_dim(pairs, mine, axis=1, keepdims=False)]
    dot_general x3, matrix products: 1.66 us -> 3.56 us  [on_device(): jnp.einsum('tco,cbo->tcb', grad_cols, weight_slot, preferred_element_type...]
  transfers between devices with their start and end apart: 3 -> 3, of which waited for: 1 -> 1; matrix products, arithmetic and copies ran while one was open for 13% -> 14% of each run, Pallas kernels for 0% -> 0%
where the time goes in v5:
time: 159 us; the launch traced here: 158 us
  blocking collectives  68.6 us (43%)
  local copies, waits for them, and re-layouts  21.8 us (14%)
  starting transfers between devices  19.7 us (12%)
  between operations  14.3 us (9%)
  waiting for transfers between devices  13.6 us (9%)
  other arithmetic  10.4 us (7%)
  matrix products  9.57 us (6%)
    all_to_all x1, blocking collectives, reduce_over_dp(): across = jnp.sum(lax.all_to_all(across, 'yh', 0, 0, tiled=True), axis=0)  39.9 us
    all_gather x1, blocking collectives, on_device(): ring = lax.all_gather(pair, 'x', axis=1, tiled=False)  23.2 us
    all_to_all x1, starting transfers between devices, reduce_over_dp(): along = lax.all_to_all(across.reshape(planes, width), 'z', 0, 0, tiled=True)  17.5 us
    all_to_all x1, waiting for transfers between devices, reduce_over_dp(): along = lax.all_to_all(across.reshape(planes, width), 'z', 0, 0, tiled=True)  13.6 us
    transpose x3, local copies, waits for them, and re-layouts, on_device(): jnp.einsum('tco,cbo->tcb', grad_cols, weight_slot, preferred_element_type...  6.5 us
    unnamed x30, local copies, waits for them, and re-layouts  5.52 us
    all_gather x1, blocking collectives, on_device(): pair = lax.all_gather(tokens, 'yl', axis=0, tiled=False)  5.5 us
    slice x1, other arithmetic, reduce_over_dp(): keep = jnp.where(first, pairs[:, 0], pairs[:, 1])  4.8 us
  transfers between devices with their start and end apart: 3, of which 1 were waited for; matrix products, arithmetic and copies ran while one was open for 14% of the time, Pallas kernels for 0%

profile of v5, /device:TPU:6, one launch (start us, length us, event | category | flops | bytes accessed | tf_op | source)
XLA Modules:
  0.0 157.9 jit_solution(10753395081641019766)
XLA Ops:
  7.2 5.5 %all-gather = bf16[256,384]{1,0:T(8,128)(2,1)S(1)} all-gather(bf16[128,384]{1,0:T(8,128)(2,1)} %param.4), channel_id=2, replica_groups=mesh['z'=16,'yh'=4,'c'=2,'yl'=2,'x'=4] {'yl'}, dimensions={0}, use_global_device_ids=true | all-gather | bytes 294912 | tf_op jit(solution)/shard_map/all_gather | solution.py:35
  12.7 23.2 %all-gather.1 = bf16[2,512,384]{2,1,0:T(8,128)(2,1)S(1)} all-gather(bf16[2,128,384]{2,1,0:T(8,128)(2,1)S(1)} %bitcast.116), channel_id=3, replica_groups=mesh['z'=16,'yh'=4,'c'=2,'yl'=2,'x'=4] {'x'}, dimensions={1}, use_global_device_ids=true | all-gather | bytes 983040 | tf_op jit(solution)/shard_map/all_gather | solution.py:36
  35.9 0.6 copy.106
  37.2 0.4 copy.123
  39.1 0.4 copy-done.11
  39.7 0.4 convolution_bitcast_fusion
  40.2 0.4 convolution_bitcast_fusion.1
  40.6 0.4 convolution_bitcast_fusion.2
  41.3 1.6 %copy.129 = f32[128,12,3,128]{3,2,1,0:T(4,128)S(1)} copy(f32[128,12,3,128]{3,0,1,2:T(8,128)S(1)} %pad_maximum_fusion) | data formatting | bytes 4718592 | tf_op jit(solution)/shard_map/stack | solution.py:76
  42.9 3.3 %reshape_reshape.7 = f32[64,2,4608]{2,1,0:T(2,128)} reshape(f32[128,12,3,128]{3,2,1,0:T(4,128)S(1)} %copy.129) | data formatting | bytes 4718592 | tf_op jit(solution)/shard_map/reshape;reshape | solution.py:15
  46.2 4.8 %fusion.36 = (f32[64,1,4608]{2,1,0:T(1,128)S(1)}, f32[64,1,4608]{2,1,0:T(1,128)S(1)}, f32[64,1,4608]{2,1,0:T(1,128)S(1)}) fusion(f32[64,2,4608]{2,1,0:T(2,128)} %reshape_reshape.7, pred[]{:T(512)S(6)} %eq.60), kind=kLoop, calls=%fused_computation.55 | loop fusion | flops 294912 | bytes 5898241 | tf_op jit(solution)/shard_map/slice | solution.py:18
  51.0 1.1 copy.164
  52.1 2.1 %collective-permute-start = (f32[64,4608]{1,0:T(8,128)}, f32[64,4608]{1,0:T(8,128)}, u32[]{:S(2)}, u32[]{:S(2)}) collective-permute-start(f32[64,4608]{1,0:T(8,128)} %bitcast.103), channel_id=1, source_target_pairs={{0,8},{8,0},{1,9},{9,1},{2,10},{10,2},{3,11},{11,3},{4,12},{12,4},... | collective-permute-start | bytes 3538952 | tf_op jit(solution)/shard_map/ppermute | solution.py:20
  54.2 1.2 convolution_bitcast_fusion.5
  55.6 2.5 %copy.116 = f32[128,12,128]{2,1,0:T(8,128)} copy(f32[128,12,128]{0,2,1:T(8,128)} %convolution_bitcast_fusion.5) | data formatting | bytes 1572864 | tf_op jit(solution)/shard_map/tco,cbo->tcb/transpose | solution.py:58
  58.2 1.4 copy.119
  59.5 2.2 %convolution_bitcast_fusion.3 = f32[128,12,128]{0,2,1:T(8,128)} fusion(bf16[128,12,128]{0,2,1:T(8,128)(2,1)S(1)} %bitcast.110, bf16[12,3,128,128]{3,2,1,0:T(8,128)(2,1)} %param.5), kind=kOutput, calls=%fused_computation.9 | convolution fusion | flops 50331648 | bytes 1572864 | tf_op jit(solution)/shard_map/tco,cbo->tcb/dot_general | solution.py:58
  61.7 2.6 %copy.122 = f32[128,12,128]{2,1,0:T(8,128)} copy(f32[128,12,128]{0,2,1:T(8,128)} %convolution_bitcast_fusion.3) | data formatting | bytes 1572864 | tf_op jit(solution)/shard_map/tco,cbo->tcb/transpose | solution.py:58
  64.3 0.9 fusion.20
  65.5 0.9 fusion.24
  66.8 1.0 add_add_fusion
  67.8 1.4 copy.163
  69.3 1.5 fusion.5
  71.5 1.4 all_to_all.16
  72.9 39.9 %all_to_all.19 = f32[4,1,73728]{2,1,0:T(1,128)S(1)} all-to-all(f32[4,1,73728]{2,1,0:T(1,128)S(1)} %all_to_all.16), channel_id=1, replica_groups=mesh['z'=16,'yh'=4,'c'=2,'yl'=2,'x'=4] {'yh'}, dimensions={0} | all-to-all | bytes 2359296 | tf_op jit(solution)/shard_map/all_to_all | solution.py:23
  112.8 2.1 %reduce_sum.18 = f32[73728]{0:T(1024)} reduce(f32[4,1,73728]{2,1,0:T(1,128)S(1)} %all_to_all.19, f32[]{:T(128)} %constant.10.clone.1), dimensions={0,1}, to_apply=%region_1.2 | reduce | flops 221184 | bytes 1474564 | tf_op jit(solution)/shard_map/reduce_sum | solution.py:23
  114.9 17.5 %all-to-all-start.1 = ((f32[16,1,4608]{2,1,0:T(1,128)}), f32[16,1,4608]{2,1,0:T(1,128)S(1)}, u32[]{:S(2)}, u32[]{:S(2)}) async-start(f32[16,1,4608]{2,1,0:T(1,128)} %bitcast.30), calls=%async_computation.2 | async-start | bytes 589824 | tf_op jit(solution)/shard_map/all_to_all | solution.py:24
  133.2 0.7 copy-done.10
  134.2 0.9 copy.137
  135.1 1.6 %convert_element_type.41 = bf16[128,384]{1,0:T(8,128)(2,1)} convert(f32[128,384]{1,0:T(8,128)} %reduce-scatter.2.cloned.1.call-done) | non-fusion elementwise | flops 49152 | bytes 294912 | tf_op jit(solution)/shard_map/convert_element_type | solution.py:72
  136.7 13.6 %all-to-all-done.1 = f32[16,1,4608]{2,1,0:T(1,128)S(1)} async-done(((f32[16,1,4608]{2,1,0:T(1,128)}), f32[16,1,4608]{2,1,0:T(1,128)S(1)}, u32[]{:S(2)}, u32[]{:S(2)}) %all-to-all-start.1) | async-done | bytes 294944 | tf_op jit(solution)/shard_map/all_to_all | solution.py:24
  150.5 0.6 mul.11
  (45 shorter events, 5.5 us)
Async XLA Ops:
  7.2 127.9 %reduce-scatter.2.cloned.1.call-start = ((), (), s32[]{:S(2)}) async-start(), calls=%async_computation.3 | async-start | bytes 1769472 | tf_op jit(solution)/shard_map/reduce_scatter | solution.py:72
  35.9 0.9 copy-start.12
  37.6 3.0 %copy-start.7 = (bf16[128,12,128]{0,2,1:T(8,128)(2,1)}, bf16[128,12,128]{0,2,1:T(8,128)(2,1)S(1)}, u32[]{:S(2)}) copy-start(bf16[128,12,128]{0,2,1:T(8,128)(2,1)S(1)} %copy.123) | copy-start | bytes 1179652
  38.3 1.8 %copy-start.5 = (bf16[128,12,128]{0,2,1:T(8,128)(2,1)}, bf16[128,12,128]{0,2,1:T(8,128)(2,1)S(1)}, u32[]{:S(2)}) copy-start(bf16[128,12,128]{0,2,1:T(8,128)(2,1)S(1)} %copy.125) | copy-start | bytes 1179652
  38.4 1.1 copy-start.11
  39.5 0.7 copy-start.9
  51.0 3.2 %copy-start = (bf16[12,3,128,128]{3,2,1,0:T(8,128)(2,1)S(1)}, bf16[12,3,128,128]{3,2,1,0:T(8,128)(2,1)}, u32[]{:S(2)}) copy-start(bf16[12,3,128,128]{3,2,1,0:T(8,128)(2,1)} %param.5) | copy-start | bytes 3538948
  52.1 17.1 %collective-permute-start = (f32[64,4608]{1,0:T(8,128)}, f32[64,4608]{1,0:T(8,128)}, u32[]{:S(2)}, u32[]{:S(2)}) collective-permute-start(f32[64,4608]{1,0:T(8,128)} %bitcast.103), channel_id=1, source_target_pairs={{0,8},{8,0},{1,9},{9,1},{2,10},{10,2},{3,11},{11,3},{4,12},{12,4},... | collective-permute-start | bytes 3538952 | tf_op jit(solution)/shard_map/ppermute | solution.py:20
  61.7 2.6 %copy-start.3 = (f32[128,12,128]{2,1,0:T(8,128)S(1)}, f32[128,12,128]{2,1,0:T(8,128)}, u32[]{:S(2)}) copy-start(f32[128,12,128]{2,1,0:T(8,128)} %copy.116) | copy-start | bytes 2359300
  64.3 1.2 copy-start.2
  65.5 1.2 copy-start.4
  112.8 19.7 %copy-start.1 = (bf16[12,3,128,128]{3,2,1,0:T(8,128)(2,1)S(1)}, bf16[12,3,128,128]{3,2,1,0:T(8,128)(2,1)}, u32[]{:S(2)}) copy-start(bf16[12,3,128,128]{3,2,1,0:T(8,128)(2,1)} %param.5) | copy-start | bytes 3538948
  112.8 19.7 %copy-start.8 = (bf16[128,12,128]{0,2,1:T(8,128)(2,1)S(1)}, bf16[128,12,128]{0,2,1:T(8,128)(2,1)}, u32[]{:S(2)}) copy-start(bf16[128,12,128]{0,2,1:T(8,128)(2,1)} %copy-done.7) | copy-start | bytes 1179652
  114.9 17.9 %copy-start.6 = (bf16[128,12,128]{0,2,1:T(8,128)(2,1)S(1)}, bf16[128,12,128]{0,2,1:T(8,128)(2,1)}, u32[]{:S(2)}) copy-start(bf16[128,12,128]{0,2,1:T(8,128)(2,1)} %copy-done.5) | copy-start | bytes 1179652
  114.9 35.3 %all-to-all-start.1 = ((f32[16,1,4608]{2,1,0:T(1,128)}), f32[16,1,4608]{2,1,0:T(1,128)S(1)}, u32[]{:S(2)}, u32[]{:S(2)}) async-start(f32[16,1,4608]{2,1,0:T(1,128)} %bitcast.30), calls=%async_computation.2 | async-start | bytes 589824 | tf_op jit(solution)/shard_map/all_to_all | solution.py:24
  132.8 1.0 copy-start.10
Sparse Core Ops, SparseCore 0:
  69.4 59.4 reduce-scatter.1
